TPU v7x, 512 devices: a whole 4x4x16 slice. The times are simulated.
512 devices in a mesh: attn: 64 (over y, z), dp: 4 (over x), tensor: 2 (over core).
Axes of the slice: x: 4, y: 4, z: 16, core: 2. Of those that a mesh axis runs over, the one named last changes fastest.
Arguments:
- hidden_state: bfloat16 [256, 8192], P('dp', 'attn'), may hold values from -6 to 6
- w_query: bfloat16 [8192, 8192], P('attn', 'tensor'), may hold values from -0.0625 to 0.0625
- w_keyval: bfloat16 [8192, 2, 1024], P('attn', None, 'tensor'), may hold values from -0.0625 to 0.0625
- w_output: bfloat16 [8192, 8192], P('tensor', 'attn'), may hold values from -0.0625 to 0.0625
- kv_cache: bfloat16 [4, 49152, 2, 8, 128], P('dp', 'attn', None, 'tensor'), as said below
- lengths: int32 [4, 64], P('dp'), may hold values from 1 to 256, 8192 in all within a row
- owner_of: int32 [4, 64, 1], P('dp'), may hold values from 0 to 63; in each aligned block of 64 rows (0 to 63, 64 to 127, ..., all dimensions but the last counted through in order) at most 3 rows name the same one
Outputs:
- attended: bfloat16 [256, 8192], P('dp', 'attn')
Inputs may be any that keep to these rules, and one draw needn't show every extreme that they name: `owner_of`: in each data group at most 3 requests are placed on one attention device, and in some groups exactly 3 on one. The lengths of each data group sum to 8192, and the longest is exactly 256. `kv_cache`: finite keys and values.
All inputs are finite; a program needn't handle non-finite values.
Results may differ from a plain program's by a relative error of at most 0.009.
The roundings to bfloat16 on the way count: a program that leaves them out, or rounds other values in their place, can miss the bound.
Values may be sent and summed in bfloat16 or wider, within the bound.
No kernel may reach another device: no remote copies, remote signals or barrier semaphores. Data moves between devices by JAX's collectives and lax.ppermute only.
A program may use at most 64 MiB of HBM per device.

v0:
```python
import math

import jax
import jax.numpy as jnp
from jax import lax
from jax.sharding import PartitionSpec as P

HD = 128
CAP = 3


ROPE_BASE = 500000.0


def rotate_pairs(vectors, positions):
    half_dim = vectors.shape[-1] // 2
    steps_f = jnp.arange(half_dim).astype(jnp.float32) * (2.0 / vectors.shape[-1])
    inv_freq = jnp.exp(-math.log(ROPE_BASE) * steps_f)
    angles = positions[:, None] * inv_freq[None, :]
    cosine = jnp.cos(angles)[:, None, :]
    sine_part = jnp.sin(angles)[:, None, :]
    front_half = vectors[..., :half_dim]
    back_half = vectors[..., half_dim:]
    return jnp.concatenate(
        [front_half * cosine - back_half * sine_part, back_half * cosine + front_half * sine_part],
        axis=-1,
    )


def finish(query_part, keyval_part, positions, heads_loc, kv_loc):
    row_count = query_part.shape[0]
    query_rot = rotate_pairs(query_part.reshape(row_count, heads_loc, HD), positions).astype(
        jnp.bfloat16
    )
    keyval = keyval_part.reshape(row_count, 2, kv_loc, HD)
    key_rot = rotate_pairs(keyval[:, 0], positions).astype(jnp.bfloat16)
    val_new = keyval[:, 1].astype(jnp.bfloat16)
    packed = jnp.stack([key_rot, val_new], axis=1).reshape(row_count, 2 * kv_loc * HD)
    return (query_rot.reshape(row_count, heads_loc * HD), packed)


def local(hidden_state, w_query, w_keyval, w_output, kv_cache, lengths, owner_of):
    rows_group = hidden_state.shape[0]
    width_loc = hidden_state.shape[1]
    my_index = lax.axis_index("attn")
    heads_loc = w_query.shape[1] // HD
    kv_loc = w_keyval.shape[2] // HD
    group_size = heads_loc // kv_loc
    score_scale = 1.0 / math.sqrt(HD)
    query_part = jnp.dot(hidden_state, w_query, preferred_element_type=jnp.float32)
    keyval_part = jnp.dot(
        hidden_state,
        w_keyval.reshape(width_loc, 2 * kv_loc * HD),
        preferred_element_type=jnp.float32,
    )
    owners = owner_of.reshape(rows_group)
    req_lens = lengths.reshape(rows_group)
    req_order = jnp.arange(rows_group, dtype=jnp.int32)
    same_owner = owners[:, None] == owners[None, :]
    earlier = req_order[None, :] < req_order[:, None]
    before_mine = same_owner & earlier
    starts = jnp.sum(jnp.where(before_mine, req_lens[None, :], 0), axis=1)
    slot_rank = jnp.sum(before_mine.astype(jnp.int32), axis=1)
    positions = req_lens.astype(jnp.float32)
    query_sum, keyval_sum = lax.psum((query_part, keyval_part), "attn")
    query_rows, keyval_rows = finish(query_sum, keyval_sum, positions, heads_loc, kv_loc)
    slot_hit = (owners[None, :] == my_index) & (
        slot_rank[None, :] == jnp.arange(CAP, dtype=jnp.int32)[:, None]
    )
    chosen = jnp.sum(jnp.where(slot_hit, req_order[None, :], 0), axis=1)
    present = jnp.any(slot_hit, axis=1)
    my_start = jnp.take(starts, chosen)
    my_len = jnp.where(present, jnp.take(req_lens, chosen), 0)
    query_mine = jnp.take(query_rows, chosen, axis=0)
    keyval_mine = jnp.take(keyval_rows, chosen, axis=0).reshape(CAP, 2, kv_loc, HD)
    cache_local = kv_cache[0]
    grouped = query_mine.reshape(CAP, kv_loc, group_size, HD)
    scores = (
        jnp.einsum("ckgd,skd->ckgs", grouped, cache_local[:, 0], preferred_element_type=jnp.float32)
        * score_scale
    )
    own_score = (
        jnp.einsum("ckgd,ckd->ckg", grouped, keyval_mine[:, 0], preferred_element_type=jnp.float32)
        * score_scale
    )
    slot_pos = jnp.arange(cache_local.shape[0], dtype=jnp.int32)
    live = (slot_pos[None, :] >= my_start[:, None]) & (
        slot_pos[None, :] < (my_start + my_len)[:, None]
    )
    live = live[:, None, None, :]
    row_max = jnp.maximum(jnp.max(jnp.where(live, scores, -jnp.inf), axis=-1), own_score)
    weights = jnp.where(live, jnp.exp(scores - row_max[..., None]), 0.0)
    own_weight = jnp.exp(own_score - row_max)
    total_weight = jnp.sum(weights, axis=-1) + own_weight
    probs = (weights / total_weight[..., None]).astype(jnp.bfloat16)
    own_prob = (own_weight / total_weight).astype(jnp.bfloat16)
    mixed = jnp.einsum(
        "ckgs,skd->ckgd", probs, cache_local[:, 1], preferred_element_type=jnp.float32
    )
    mixed = (
        mixed
        + own_prob.astype(jnp.float32)[..., None]
        * keyval_mine[:, 1].astype(jnp.float32)[:, :, None, :]
    )
    out_slots = mixed.reshape(CAP, heads_loc * HD).astype(jnp.bfloat16)
    gathered = lax.all_gather(out_slots, "attn", axis=0, tiled=True)
    heads_out = jnp.take(gathered, owners * CAP + slot_rank, axis=0)
    out_part = jnp.dot(heads_out, w_output, preferred_element_type=jnp.float32)
    out_total = lax.psum(out_part, "tensor")
    return out_total.astype(jnp.bfloat16)


def solution(mesh):
    placed = (
        P("dp", "attn"),
        P("attn", "tensor"),
        P("attn", None, "tensor"),
        P("tensor", "attn"),
        P("dp", "attn", None, "tensor", None),
        P("dp", None),
        P("dp", None, None),
    )
    return jax.shard_map(
        local, mesh=mesh, in_specs=placed, out_specs=P("dp", "attn"), check_vma=False
    )
```

profile of v0, /device:TPU:1, one launch (start us, length us, event | category | flops | bytes accessed | tf_op | source)
XLA Modules:
  0.0 454.5 jit_solution(9612542293275163695)
XLA Ops:
  6.5 1.2 copy-done
  7.8 1.0 convolution_bitcast_fusion
  8.8 1.2 copy.37
  10.0 0.2 fusion.30
  10.2 0.8 reshape.238
  11.1 0.2 select_reduce_fusion.1
  11.3 0.1 select_reduce_fusion.2
  11.5 0.6 gather_fusion.4
  12.1 0.6 gather_fusion.3
  12.8 1.4 copy.65
  14.1 0.1 fusion.24
  14.4 0.2 multiply_cosine_fusion
  14.6 269.9 %all-reduce.3.cloned.1.call-done = (f32[64,32,128]{2,1,0:T(8,128)}, f32[64,2,4,128]{3,2,1,0:T(4,128)}) async-done(((f32[64,32,128]{2,1,0:T(8,128)}, f32[64,2,4,128]{3,2,1,0:T(4,128)}), (f32[64,32,128]{2,1,0:T(8,128)}, f32[64,2,4,128]{3,2,1,0:T(4,128)})) %all-reduce.3.cloned.1.call-update) | async-done | bytes 1310736 | tf_op jit(solution)/shard_map/psum | solution.py:65
  284.5 1.0 slice_bitcast_fusion.4
  285.5 0.9 slice.87
  286.4 0.2 fusion.12
  286.6 0.1 pad_maximum_fusion.1
  286.8 0.6 gather_fusion.1
  287.5 0.5 subtract_convert_fusion
  288.0 0.3 pad_maximum_fusion
  288.3 0.2 copy.66
  288.5 0.6 gather_fusion
  289.1 0.1 fusion.15
  289.4 0.4 select_reduce_fusion
  289.8 0.2 fusion.7
  290.0 0.3 fusion.2
  290.3 0.6 reshape.283
  291.0 136.5 %all-gather.3.cloned.1.call-done = bf16[64,3,4096]{2,1,0:T(4,128)(2,1)} async-done(((bf16[1,3,4096]{2,1,0:T(4,128)(2,1)}), bf16[64,3,4096]{2,1,0:T(4,128)(2,1)}) %all-gather.3.cloned.1.call-update) | async-done | bytes 1572880 | tf_op jit(solution)/shard_map/all_gather | solution.py:106
  427.5 3.1 reshape.284
  430.6 0.9 gather_fusion.2
  431.5 1.6 fusion.3
  433.1 14.6 %psum.23 = bf16[64,128]{1,0:T(8,128)(2,1)} all-reduce(f32[64,128]{1,0:T(8,128)S(1)} %fusion.3), channel_id=1, replica_groups=mesh['attn'=64,'dp'=4,'tensor'=2] {'tensor'}, use_global_device_ids=true, to_apply=%region_8.10 | all-reduce | flops 8192 | bytes 49152 | tf_op jit(solution)/shard_map/psum | solution.py:109
  (39 shorter events, 0.7 us)
Async XLA Ops:
  6.5 1.2 copy-start
  6.5 277.9 %all-reduce.3.cloned.1.call-start = ((), (), s32[]{:S(2)}) async-start(), calls=%async_computation.1 | async-start | bytes 2621440 | tf_op jit(solution)/shard_map/psum | solution.py:65
  8.8 1.2 copy-start.5
  8.8 1.2 copy-start.6
  10.0 1.1 copy-start.1
  10.0 1.2 copy-start.7
  10.2 2.6 copy-start.4
  11.1 416.4 %all-gather.3.cloned.1.call-start = ((), (), s32[]{:S(2)}) async-start(), calls=%async_computation | async-start | bytes 2129920 | tf_op jit(solution)/shard_map/all_gather | solution.py:106
  284.5 3.0 copy-start.2
  287.9 1.4 copy-start.3
Sparse Core Ops, SparseCore 0:
  11.2 273.2 all-reduce.2
  291.1 136.3 all-gather.2
where the time goes:
time: 455 us
  waiting for transfers between devices  406 us (89%)
  blocking collectives  14.6 us (3%)
  local copies, waits for them, and re-layouts  14 us (3%)
  between operations  13.7 us (3%)
    psum x1, waiting for transfers between devices, local(): query_sum, keyval_sum = lax.psum((query_part, keyval_part), 'attn')  270 us
    all_gather x1, waiting for transfers between devices, local(): gathered = lax.all_gather(out_slots, 'attn', axis=0, tiled=True)  137 us
    psum x1, blocking collectives, local(): out_total = lax.psum(out_part, 'tensor')  14.6 us
  transfers between devices with their start and end apart: 2, of which 2 were waited for; matrix products, arithmetic and copies ran while one was open for 1% of the time, Pallas kernels for 0%

commit v1 on v0

--- a/solution.py
+++ b/solution.py
@@ -3,10 +3,12 @@
 import jax
 import jax.numpy as jnp
 from jax import lax
+from jax.sharding import Mesh
 from jax.sharding import PartitionSpec as P
 
 HD = 128
 CAP = 3
+Y_PARTS = 4
 
 
 ROPE_BASE = 500000.0
@@ -27,43 +29,53 @@
     )
 
 
-def finish(query_part, keyval_part, positions, heads_loc, kv_loc):
-    row_count = query_part.shape[0]
-    query_rot = rotate_pairs(query_part.reshape(row_count, heads_loc, HD), positions).astype(
-        jnp.bfloat16
-    )
-    keyval = keyval_part.reshape(row_count, 2, kv_loc, HD)
-    key_rot = rotate_pairs(keyval[:, 0], positions).astype(jnp.bfloat16)
-    val_new = keyval[:, 1].astype(jnp.bfloat16)
-    packed = jnp.stack([key_rot, val_new], axis=1).reshape(row_count, 2 * kv_loc * HD)
-    return (query_rot.reshape(row_count, heads_loc * HD), packed)
+def gather_rows(rows, n_y, n_z):
+    stage = lax.all_to_all(jnp.tile(rows[None], (n_z, 1, 1)), "az", 0, 0, tiled=True)
+    stage = lax.all_to_all(jnp.tile(stage[None], (n_y, 1, 1, 1)), "ay", 0, 0, tiled=True)
+    return stage.reshape((n_y * n_z * rows.shape[0],) + rows.shape[1:])
 
 
-def local(hidden_state, w_query, w_keyval, w_output, kv_cache, lengths, owner_of):
+def local(hidden_state, w_query, w_keyval, w_output, kv_cache, lengths, owner_of, n_y, n_z):
     rows_group = hidden_state.shape[0]
     width_loc = hidden_state.shape[1]
-    my_index = lax.axis_index("attn")
+    my_index = lax.axis_index("ay") * n_z + lax.axis_index("az")
     heads_loc = w_query.shape[1] // HD
     kv_loc = w_keyval.shape[2] // HD
     group_size = heads_loc // kv_loc
+    q_cols = heads_loc * HD
+    kv_cols = kv_loc * HD
     score_scale = 1.0 / math.sqrt(HD)
     query_part = jnp.dot(hidden_state, w_query, preferred_element_type=jnp.float32)
     keyval_part = jnp.dot(
         hidden_state,
-        w_keyval.reshape(width_loc, 2 * kv_loc * HD),
+        w_keyval.reshape(width_loc, 2 * kv_cols),
         preferred_element_type=jnp.float32,
     )
+    both = jnp.concatenate([query_part, keyval_part], axis=1)
+    cols = both.shape[1]
+    per_y = rows_group // n_y
+    part = lax.all_to_all(both.reshape(n_y, per_y, cols), "ay", 0, 0, tiled=True).sum(0)
+    part = lax.all_to_all(part.reshape(n_z, per_y // n_z, cols), "az", 0, 0, tiled=True).sum(0)
     owners = owner_of.reshape(rows_group)
     req_lens = lengths.reshape(rows_group)
+    mine_pos = lax.dynamic_slice(req_lens, (my_index,), (1,)).astype(jnp.float32)
+    q_rot = rotate_pairs(part[:, :q_cols].reshape(1, heads_loc, HD), mine_pos).astype(jnp.bfloat16)
+    k_rot = rotate_pairs(part[:, q_cols : q_cols + kv_cols].reshape(1, kv_loc, HD), mine_pos).astype(
+        jnp.bfloat16
+    )
+    v_new = part[:, q_cols + kv_cols :].astype(jnp.bfloat16)
+    row_bf = jnp.concatenate(
+        [q_rot.reshape(1, q_cols), k_rot.reshape(1, kv_cols), v_new.reshape(1, kv_cols)], axis=1
+    )
+    all_rows = gather_rows(row_bf, n_y, n_z)
+    query_rows = all_rows[:, :q_cols]
+    keyval_rows = all_rows[:, q_cols:]
     req_order = jnp.arange(rows_group, dtype=jnp.int32)
     same_owner = owners[:, None] == owners[None, :]
     earlier = req_order[None, :] < req_order[:, None]
     before_mine = same_owner & earlier
     starts = jnp.sum(jnp.where(before_mine, req_lens[None, :], 0), axis=1)
     slot_rank = jnp.sum(before_mine.astype(jnp.int32), axis=1)
-    positions = req_lens.astype(jnp.float32)
-    query_sum, keyval_sum = lax.psum((query_part, keyval_part), "attn")
-    query_rows, keyval_rows = finish(query_sum, keyval_sum, positions, heads_loc, kv_loc)
     slot_hit = (owners[None, :] == my_index) & (
         slot_rank[None, :] == jnp.arange(CAP, dtype=jnp.int32)[:, None]
     )
@@ -103,7 +115,7 @@
         * keyval_mine[:, 1].astype(jnp.float32)[:, :, None, :]
     )
     out_slots = mixed.reshape(CAP, heads_loc * HD).astype(jnp.bfloat16)
-    gathered = lax.all_gather(out_slots, "attn", axis=0, tiled=True)
+    gathered = gather_rows(out_slots, n_y, n_z)
     heads_out = jnp.take(gathered, owners * CAP + slot_rank, axis=0)
     out_part = jnp.dot(heads_out, w_output, preferred_element_type=jnp.float32)
     out_total = lax.psum(out_part, "tensor")
@@ -111,15 +123,23 @@
 
 
 def solution(mesh):
+    n_attn = mesh.shape["attn"]
+    n_y = Y_PARTS if n_attn % Y_PARTS == 0 else 1
+    n_z = n_attn // n_y
+    devs = mesh.devices
+    sub = Mesh(devs.reshape((n_y, n_z) + devs.shape[1:]), ("ay", "az") + tuple(mesh.axis_names[1:]))
+    A = ("ay", "az")
     placed = (
-        P("dp", "attn"),
-        P("attn", "tensor"),
-        P("attn", None, "tensor"),
-        P("tensor", "attn"),
-        P("dp", "attn", None, "tensor", None),
+        P("dp", A),
+        P(A, "tensor"),
+        P(A, None, "tensor"),
+        P("tensor", A),
+        P("dp", A, None, "tensor", None),
         P("dp", None),
         P("dp", None, None),
     )
-    return jax.shard_map(
-        local, mesh=mesh, in_specs=placed, out_specs=P("dp", "attn"), check_vma=False
-    )
+
+    def body(*args):
+        return local(*args, n_y=n_y, n_z=n_z)
+
+    return jax.shard_map(body, mesh=sub, in_specs=placed, out_specs=P("dp", A), check_vma=False)

time: 455 us -> 170 us (0.37)
  the two profiles are of different devices: /device:TPU:1 before, /device:TPU:35 now
where the time goes in v1:
time: 170 us; the launch traced here: 169 us
  blocking collectives  63.6 us (37%)
  waiting for transfers between devices  49.3 us (29%)
  starting transfers between devices  28.6 us (17%)
  local copies, waits for them, and re-layouts  19.3 us (11%)
  other arithmetic  4.63 us (3%)
  matrix products  3.6 us (2%)
    all_to_all x1, blocking collectives, gather_rows(): lax.all_to_all(jnp.tile(rows[None], (n_z, 1, 1)), 'az', 0, 0, tiled=True)  32 us
    all_to_all x1, blocking collectives, local(): lax.all_to_all(both.reshape(n_y, per_y, cols), 'ay', 0, 0, tiled=True)  21 us
    all_to_all x2, waiting for transfers between devices, gather_rows(): lax.all_to_all(jnp.tile(stage[None], (n_y, 1, 1, 1)), 'ay', 0, 0, tiled=T...  20.1 us
    all_to_all x1, waiting for transfers between devices, local(): lax.all_to_all(part.reshape(n_z, per_y // n_z, cols), 'az', 0, 0, tiled=T...  17.9 us
    all_to_all x1, starting transfers between devices, local(): lax.all_to_all(part.reshape(n_z, per_y // n_z, cols), 'az', 0, 0, tiled=T...  14.7 us
    all_to_all x1, waiting for transfers between devices, gather_rows(): lax.all_to_all(jnp.tile(rows[None], (n_z, 1, 1)), 'az', 0, 0, tiled=True)  11.3 us
    psum x1, blocking collectives, local(): out_total = lax.psum(out_part, 'tensor')  10.6 us
    all_to_all x2, starting transfers between devices, gather_rows(): lax.all_to_all(jnp.tile(stage[None], (n_y, 1, 1, 1)), 'ay', 0, 0, tiled=T...  7.04 us
  transfers between devices with their start and end apart: 4, of which 4 were waited for; matrix products, arithmetic and copies ran while one was open for 3% of the time, Pallas kernels for 0%

profile of v1, /device:TPU:35, one launch (start us, length us, event | category | flops | bytes accessed | tf_op | source)
XLA Modules:
  0.0 169.3 jit_solution(740703120776381159)
XLA Ops:
  0.0 1.1 copy.43
  1.3 1.0 fusion.31
  2.6 21.0 %all_to_all.30 = f32[4,16,5120]{2,1,0:T(8,128)S(1)} all-to-all(f32[4,16,5120]{2,1,0:T(8,128)S(1)} %bitcast.107), channel_id=1, replica_groups=mesh['ay'=4,'az'=16,'dp'=4,'tensor'=2] {'ay'}, dimensions={0} | all-to-all | bytes 2621440 | tf_op jit(solution)/shard_map/all_to_all | solution.py:57
  23.7 0.9 reshape.240
  24.7 14.7 %all-to-all-start.1 = ((f32[16,1,5120]{2,1,0:T(1,128)}), f32[16,1,5120]{2,1,0:T(1,128)S(1)}, u32[]{:S(2)}, u32[]{:S(2)}) async-start(f32[16,1,5120]{2,1,0:T(1,128)} %reshape.240), calls=%async_computation.1 | async-start | bytes 655360 | tf_op jit(solution)/shard_map/all_to_all | solution.py:58
  39.3 0.6 fusion.30
  39.9 0.7 fusion.26
  40.9 17.9 %all-to-all-done.1 = f32[16,1,5120]{2,1,0:T(1,128)S(1)} async-done(((f32[16,1,5120]{2,1,0:T(1,128)}), f32[16,1,5120]{2,1,0:T(1,128)S(1)}, u32[]{:S(2)}, u32[]{:S(2)}) %all-to-all-start.1) | async-done | bytes 327712 | tf_op jit(solution)/shard_map/all_to_all | solution.py:58
  59.7 0.5 broadcast.212
  60.2 1.6 reduce.3
  61.9 0.8 reshape.297
  62.6 6.9 %all-to-all-start.2 = ((bf16[16,2,2560]{2,1,0:T(2,128)(2,1)}), bf16[16,2,2560]{2,1,0:T(2,128)(2,1)S(1)}, u32[]{:S(2)}, u32[]{:S(2)}) async-start(bf16[16,2,2560]{2,1,0:T(2,128)(2,1)} %reshape.297), calls=%async_computation.2 | async-start | bytes 327680 | tf_op jit(solution)/shard_map/all_to_all | solution.py:33
  69.5 0.6 gather_fusion.3
  70.3 11.3 %all-to-all-done.2 = bf16[16,2,2560]{2,1,0:T(2,128)(2,1)S(1)} async-done(((bf16[16,2,2560]{2,1,0:T(2,128)(2,1)}), bf16[16,2,2560]{2,1,0:T(2,128)(2,1)S(1)}, u32[]{:S(2)}, u32[]{:S(2)}) %all-to-all-start.2) | async-done | bytes 163872 | tf_op jit(solution)/shard_map/all_to_all | solution.py:33
  81.8 0.9 tile.15
  82.6 3.5 %all-to-all-start.3 = ((bf16[4,16,1,5120]{3,1,2,0:T(8,128)(2,1)}), bf16[4,16,1,5120]{3,1,2,0:T(8,128)(2,1)S(1)}, u32[]{:S(2)}, u32[]{:S(2)}) async-start(bf16[4,16,1,5120]{3,1,2,0:T(8,128)(2,1)} %tile.15), calls=%async_computation.3 | async-start | bytes 1310720 | tf_op jit(solution)/shard_map/all_to_all | solution.py:34
  86.1 0.6 gather_fusion.4
  86.8 1.6 copy.76
  88.5 5.2 %all-to-all-done.3 = bf16[4,16,1,5120]{3,1,2,0:T(8,128)(2,1)S(1)} async-done(((bf16[4,16,1,5120]{3,1,2,0:T(8,128)(2,1)}), bf16[4,16,1,5120]{3,1,2,0:T(8,128)(2,1)S(1)}, u32[]{:S(2)}, u32[]{:S(2)}) %all-to-all-start.3) | async-done | bytes 655392 | tf_op jit(solution)/shard_map/all_to_all | solution.py:34
  93.7 0.8 slice.68
  94.6 1.7 %gather_fusion = bf16[3,4096]{1,0:T(4,128)(2,1)S(1)} fusion(bf16[64,4096]{1,0:T(8,128)(2,1)} %slice.68, s32[1024]{0:T(1024)S(1)} %pad_clamp_fusion.1), kind=kCustom, calls=%fused_computation.2 | custom fusion | bytes 49164 | tf_op jit(solution)/shard_map/jit(_take)/gather | solution.py:86
  96.4 0.6 gather_fusion.1
  97.1 0.4 select_reduce_fusion
  98.3 32.0 %all_to_all.31 = bf16[16,3,4096]{2,1,0:T(4,128)(2,1)S(1)} all-to-all(bf16[16,3,4096]{2,1,0:T(4,128)(2,1)S(1)} %tile.32), channel_id=1, replica_groups=mesh['ay'=4,'az'=16,'dp'=4,'tensor'=2] {'az'}, dimensions={0} | all-to-all | bytes 786432 | tf_op jit(solution)/shard_map/all_to_all | solution.py:33
  130.6 1.3 tile.33
  132.0 3.6 %all-to-all-start.5 = ((bf16[4,16,3,4096]{3,1,2,0:T(8,128)(2,1)}), bf16[4,16,3,4096]{3,1,2,0:T(8,128)(2,1)S(1)}, u32[]{:S(2)}, u32[]{:S(2)}) async-start(bf16[4,16,3,4096]{3,1,2,0:T(8,128)(2,1)} %tile.33), calls=%async_computation.5 | async-start | bytes 3145728 | tf_op jit(solution)/shard_map/all_to_all | solution.py:34
  135.6 14.8 %all-to-all-done.5 = bf16[4,16,3,4096]{3,1,2,0:T(8,128)(2,1)S(1)} async-done(((bf16[4,16,3,4096]{3,1,2,0:T(8,128)(2,1)}), bf16[4,16,3,4096]{3,1,2,0:T(8,128)(2,1)S(1)}, u32[]{:S(2)}, u32[]{:S(2)}) %all-to-all-start.5) | async-done | bytes 1572896 | tf_op jit(solution)/shard_map/all_to_all | solution.py:34
  150.4 2.7 %copy.36 = bf16[4,16,3,4096]{3,2,1,0:T(4,128)(2,1)} copy(bf16[4,16,3,4096]{3,1,2,0:T(8,128)(2,1)S(1)} %all-to-all-done.5) | data formatting | bytes 3145728 | tf_op jit(solution)/shard_map/all_to_all | solution.py:34
  153.1 3.1 %reshape.244 = bf16[192,4096]{1,0:T(8,128)(2,1)S(1)} reshape(bf16[4,16,3,4096]{3,2,1,0:T(4,128)(2,1)} %copy.36) | data formatting | bytes 3145728 | tf_op jit(solution)/shard_map/reshape | solution.py:35
  156.3 0.9 gather_fusion.2
  157.1 1.6 fusion.3
  158.7 10.6 %psum.7 = bf16[64,128]{1,0:T(8,128)(2,1)} all-reduce(f32[64,128]{1,0:T(8,128)S(1)} %fusion.3), channel_id=1, replica_groups=mesh['ay'=4,'az'=16,'dp'=4,'tensor'=2] {'tensor'}, use_global_device_ids=true, to_apply=%region_8.10 | all-reduce | flops 8192 | bytes 49152 | tf_op jit(solution)/shard_map/psum | solution.py:121
  (51 shorter events, 3.5 us)
Async XLA Ops:
  0.0 1.3 copy-start
  0.0 2.3 %copy-start.2 = (bf16[64,128]{1,0:T(8,128)(2,1)S(1)}, bf16[64,128]{1,0:T(8,128)(2,1)}, u32[]{:S(2)}) copy-start(bf16[64,128]{1,0:T(8,128)(2,1)} %param.9) | copy-start | bytes 49156
  23.6 15.7 %copy-start.1 = (s32[1,64]{1,0:T(1,128)S(1)}, s32[1,64]{1,0:T(1,128)}, u32[]{:S(2)}) copy-start(s32[1,64]{1,0:T(1,128)} %param.14) | copy-start | bytes 772
  23.6 17.0 %copy-start.3 = (s32[1,64,1]{1,2,0:T(1,128)S(1)}, s32[1,64,1]{1,2,0:T(1,128)}, u32[]{:S(2)}) copy-start(s32[1,64,1]{1,2,0:T(1,128)} %param.15) | copy-start | bytes 772
  24.7 34.2 %all-to-all-start.1 = ((f32[16,1,5120]{2,1,0:T(1,128)}), f32[16,1,5120]{2,1,0:T(1,128)S(1)}, u32[]{:S(2)}, u32[]{:S(2)}) async-start(f32[16,1,5120]{2,1,0:T(1,128)} %reshape.240), calls=%async_computation.1 | async-start | bytes 655360 | tf_op jit(solution)/shard_map/all_to_all | solution.py:58
  62.6 19.0 %all-to-all-start.2 = ((bf16[16,2,2560]{2,1,0:T(2,128)(2,1)}), bf16[16,2,2560]{2,1,0:T(2,128)(2,1)S(1)}, u32[]{:S(2)}, u32[]{:S(2)}) async-start(bf16[16,2,2560]{2,1,0:T(2,128)(2,1)} %reshape.297), calls=%async_computation.2 | async-start | bytes 327680 | tf_op jit(solution)/shard_map/all_to_all | solution.py:33
  82.6 11.1 %all-to-all-start.3 = ((bf16[4,16,1,5120]{3,1,2,0:T(8,128)(2,1)}), bf16[4,16,1,5120]{3,1,2,0:T(8,128)(2,1)S(1)}, u32[]{:S(2)}, u32[]{:S(2)}) async-start(bf16[4,16,1,5120]{3,1,2,0:T(8,128)(2,1)} %tile.15), calls=%async_computation.3 | async-start | bytes 1310720 | tf_op jit(solution)/shard_map/all_to_all | solution.py:34
  132.0 18.4 %all-to-all-start.5 = ((bf16[4,16,3,4096]{3,1,2,0:T(8,128)(2,1)}), bf16[4,16,3,4096]{3,1,2,0:T(8,128)(2,1)S(1)}, u32[]{:S(2)}, u32[]{:S(2)}) async-start(bf16[4,16,3,4096]{3,1,2,0:T(8,128)(2,1)} %tile.33), calls=%async_computation.5 | async-start | bytes 3145728 | tf_op jit(solution)/shard_map/all_to_all | solution.py:34

commit v2 on v1

--- a/solution.py
+++ b/solution.py
@@ -55,7 +55,8 @@
     cols = both.shape[1]
     per_y = rows_group // n_y
     part = lax.all_to_all(both.reshape(n_y, per_y, cols), "ay", 0, 0, tiled=True).sum(0)
-    part = lax.all_to_all(part.reshape(n_z, per_y // n_z, cols), "az", 0, 0, tiled=True).sum(0)
+    part = lax.all_to_all(part.reshape(n_z, cols // HD, HD), "az", 0, 0, tiled=True).sum(0)
+    part = part.reshape(1, cols)
     owners = owner_of.reshape(rows_group)
     req_lens = lengths.reshape(rows_group)
     mine_pos = lax.dynamic_slice(req_lens, (my_index,), (1,)).astype(jnp.float32)
@@ -67,7 +68,7 @@
     row_bf = jnp.concatenate(
         [q_rot.reshape(1, q_cols), k_rot.reshape(1, kv_cols), v_new.reshape(1, kv_cols)], axis=1
     )
-    all_rows = gather_rows(row_bf, n_y, n_z)
+    all_rows = gather_rows(row_bf.reshape(cols // HD, HD), n_y, n_z).reshape(-1, cols)
     query_rows = all_rows[:, :q_cols]
     keyval_rows = all_rows[:, q_cols:]
     req_order = jnp.arange(rows_group, dtype=jnp.int32)
@@ -115,7 +116,9 @@
         * keyval_mine[:, 1].astype(jnp.float32)[:, :, None, :]
     )
     out_slots = mixed.reshape(CAP, heads_loc * HD).astype(jnp.bfloat16)
-    gathered = gather_rows(out_slots, n_y, n_z)
+    lanes = out_slots.size // 16
+    gathered = gather_rows(out_slots.reshape(16, lanes), n_y, n_z)
+    gathered = gathered.reshape(-1, heads_loc * HD)
     heads_out = jnp.take(gathered, owners * CAP + slot_rank, axis=0)
     out_part = jnp.dot(heads_out, w_output, preferred_element_type=jnp.float32)
     out_total = lax.psum(out_part, "tensor")

time: 170 us -> 159 us (0.935)
  blocking collectives: 63.6 us -> 57.5 us
  local copies, waits for them, and re-layouts: 19.3 us -> 13.4 us
  waiting for transfers between devices: 49.3 us -> 51.2 us
  other arithmetic: 4.63 us -> 2.81 us
    all_to_all x1, blocking collectives: 32 us -> 27.7 us  [gather_rows(): lax.all_to_all(jnp.tile(rows[None], (n_z, 1, 1)), 'az', 0, 0, tiled=True)]
    reshape x2 -> x0, local copies, waits for them, and re-layouts: 4.07 us -> none  [the longest x1 3.14 us: gather_rows(): return stage.reshape((n_y * n_z * rows.shape[0],) + rows.shape[1:])]
    another operation x0 -> x1, local copies, waits for them, and re-layouts: none -> 3.26 us  [local(): gathered = gathered.reshape(-1, heads_loc * HD)]
    all_to_all x2 -> x0, local copies, waits for them, and re-layouts: 3.01 us -> none  [the longest x1 2.72 us: gather_rows(): lax.all_to_all(jnp.tile(stage[None], (n_y, 1, 1, 1)), 'ay', 0, 0, tiled=T...]
    all_to_all x2, waiting for transfers between devices: 20.1 us -> 22 us  [gather_rows(): lax.all_to_all(jnp.tile(stage[None], (n_y, 1, 1, 1)), 'ay', 0, 0, tiled=T...]
    psum x1, blocking collectives: 10.6 us -> 8.78 us  [local(): out_total = lax.psum(out_part, 'tensor')]
    unnamed x16 -> x14, local copies, waits for them, and re-layouts: 3.9 us -> 3.8 us
where the time goes in v2:
time: 159 us; the launch traced here: 158 us
  blocking collectives  57.5 us (36%)
  waiting for transfers between devices  51.2 us (32%)
  starting transfers between devices  29.3 us (18%)
  local copies, waits for them, and re-layouts  13.4 us (8%)
  matrix products  3.59 us (2%)
  other arithmetic  2.81 us (2%)
    all_to_all x1, blocking collectives, gather_rows(): lax.all_to_all(jnp.tile(rows[None], (n_z, 1, 1)), 'az', 0, 0, tiled=True)  27.7 us
    all_to_all x2, waiting for transfers between devices, gather_rows(): lax.all_to_all(jnp.tile(stage[None], (n_y, 1, 1, 1)), 'ay', 0, 0, tiled=T...  22 us
    all_to_all x1, blocking collectives, local(): lax.all_to_all(both.reshape(n_y, per_y, cols), 'ay', 0, 0, tiled=True)  21 us
    all_to_all x1, waiting for transfers between devices, local(): lax.all_to_all(part.reshape(n_z, cols // HD, HD), 'az', 0, 0, tiled=True)  17.9 us
    all_to_all x1, starting transfers between devices, local(): lax.all_to_all(part.reshape(n_z, cols // HD, HD), 'az', 0, 0, tiled=True)  14.7 us
    all_to_all x1, waiting for transfers between devices, gather_rows(): lax.all_to_all(jnp.tile(rows[None], (n_z, 1, 1)), 'az', 0, 0, tiled=True)  11.3 us
    psum x1, blocking collectives, local(): out_total = lax.psum(out_part, 'tensor')  8.78 us
    all_to_all x2, starting transfers between devices, gather_rows(): lax.all_to_all(jnp.tile(stage[None], (n_y, 1, 1, 1)), 'ay', 0, 0, tiled=T...  7.82 us
  transfers between devices with their start and end apart: 4, of which 4 were waited for; matrix products, arithmetic and copies ran while one was open for 3% of the time, Pallas kernels for 0%

profile of v2, /device:TPU:35, one launch (start us, length us, event | category | flops | bytes accessed | tf_op | source)
XLA Modules:
  0.0 158.1 jit_solution(11330362015160811168)
XLA Ops:
  0.0 1.1 copy.24
  1.1 0.2 copy-done
  1.3 1.0 fusion.31
  2.6 21.0 %all_to_all.30 = f32[4,16,5120]{2,1,0:T(8,128)S(1)} all-to-all(f32[4,16,5120]{2,1,0:T(8,128)S(1)} %bitcast.108), channel_id=1, replica_groups=mesh['ay'=4,'az'=16,'dp'=4,'tensor'=2] {'ay'}, dimensions={0} | all-to-all | bytes 2621440 | tf_op jit(solution)/shard_map/all_to_all | solution.py:57
  23.7 0.8 copy.25
  24.5 14.7 %all-to-all-start.1 = ((f32[16,40,128]{2,1,0:T(8,128)}), f32[16,40,128]{2,1,0:T(8,128)S(1)}, u32[]{:S(2)}, u32[]{:S(2)}) async-start(f32[16,40,128]{2,1,0:T(8,128)} %bitcast.33), calls=%async_computation.1 | async-start | bytes 655360 | tf_op jit(solution)/shard_map/all_to_all | solution.py:58
  39.2 0.6 fusion.30
  39.7 0.7 fusion.26
  40.5 0.2 select_reduce_fusion.1
  40.8 17.9 %all-to-all-done.1 = f32[16,40,128]{2,1,0:T(8,128)S(1)} async-done(((f32[16,40,128]{2,1,0:T(8,128)}), f32[16,40,128]{2,1,0:T(8,128)S(1)}, u32[]{:S(2)}, u32[]{:S(2)}) %all-to-all-start.1) | async-done | bytes 327712 | tf_op jit(solution)/shard_map/all_to_all | solution.py:58
  59.2 0.7 tile.11
  59.9 6.9 %all-to-all-start.2 = ((bf16[16,40,128]{2,1,0:T(8,128)(2,1)}), bf16[16,40,128]{2,1,0:T(8,128)(2,1)S(1)}, u32[]{:S(2)}, u32[]{:S(2)}) async-start(bf16[16,40,128]{2,1,0:T(8,128)(2,1)} %tile.11), calls=%async_computation.2 | async-start | bytes 327680 | tf_op jit(solution)/shard_map/all_to_all | solution.py:33
  66.7 0.6 gather_fusion.3
  67.5 11.3 %all-to-all-done.2 = bf16[16,40,128]{2,1,0:T(8,128)(2,1)S(1)} async-done(((bf16[16,40,128]{2,1,0:T(8,128)(2,1)}), bf16[16,40,128]{2,1,0:T(8,128)(2,1)S(1)}, u32[]{:S(2)}, u32[]{:S(2)}) %all-to-all-start.2) | async-done | bytes 163872 | tf_op jit(solution)/shard_map/all_to_all | solution.py:33
  78.8 0.9 tile.12
  79.7 3.5 %all-to-all-start.3 = ((bf16[4,16,40,128]{3,2,1,0:T(8,128)(2,1)}), bf16[4,16,40,128]{3,2,1,0:T(8,128)(2,1)S(1)}, u32[]{:S(2)}, u32[]{:S(2)}) async-start(bf16[4,16,40,128]{3,2,1,0:T(8,128)(2,1)} %tile.12), calls=%async_computation.3 | async-start | bytes 1310720 | tf_op jit(solution)/shard_map/all_to_all | solution.py:34
  83.2 0.6 gather_fusion.4
  83.9 1.6 %copy.56 = bf16[1,768,2,4,128]{4,1,3,2,0:T(8,128)(2,1)S(1)} copy(bf16[1,768,2,4,128]{4,3,2,1,0:T(4,128)(2,1)} %param.13) | data formatting | bytes 3145728 | tf_op args[4]
  85.6 5.2 %all-to-all-done.3 = bf16[4,16,40,128]{3,2,1,0:T(8,128)(2,1)S(1)} async-done(((bf16[4,16,40,128]{3,2,1,0:T(8,128)(2,1)}), bf16[4,16,40,128]{3,2,1,0:T(8,128)(2,1)S(1)}, u32[]{:S(2)}, u32[]{:S(2)}) %all-to-all-start.3) | async-done | bytes 655392 | tf_op jit(solution)/shard_map/all_to_all | solution.py:34
  91.0 0.6 gather_fusion
  91.6 0.6 gather_fusion.1
  92.4 0.4 select_reduce_fusion
  92.8 0.2 fusion.7
  93.1 0.3 fusion.2
  93.5 27.7 %all_to_all.31 = bf16[16,16,768]{2,1,0:T(8,128)(2,1)S(1)} all-to-all(bf16[16,16,768]{2,1,0:T(8,128)(2,1)S(1)} %tile.13), channel_id=1, replica_groups=mesh['ay'=4,'az'=16,'dp'=4,'tensor'=2] {'az'}, dimensions={0} | all-to-all | bytes 786432 | tf_op jit(solution)/shard_map/all_to_all | solution.py:33
  121.1 1.3 tile.14
  122.4 4.3 %all-to-all-start.5 = ((bf16[4,16,16,768]{3,2,1,0:T(8,128)(2,1)}), bf16[4,16,16,768]{3,2,1,0:T(8,128)(2,1)}, u32[]{:S(2)}, u32[]{:S(2)}) async-start(bf16[4,16,16,768]{3,2,1,0:T(8,128)(2,1)} %tile.14), calls=%async_computation.5 | async-start | bytes 3145728 | tf_op jit(solution)/shard_map/all_to_all | solution.py:34
  126.8 16.7 %all-to-all-done.5 = bf16[4,16,16,768]{3,2,1,0:T(8,128)(2,1)} async-done(((bf16[4,16,16,768]{3,2,1,0:T(8,128)(2,1)}), bf16[4,16,16,768]{3,2,1,0:T(8,128)(2,1)}, u32[]{:S(2)}, u32[]{:S(2)}) %all-to-all-start.5) | async-done | bytes 1572896 | tf_op jit(solution)/shard_map/all_to_all | solution.py:34
  143.5 3.3 %reshape_reshape.7 = bf16[192,4096]{1,0:T(8,128)(2,1)S(1)} reshape(bf16[4,16,16,768]{3,2,1,0:T(8,128)(2,1)} %all-to-all-done.5) | data formatting | bytes 3145728 | tf_op jit(solution)/shard_map/reshape;reshape | solution.py:121
  146.8 0.9 gather_fusion.2
  147.7 1.6 %fusion.3 = f32[64,128]{1,0:T(8,128)S(1)} fusion(bf16[4096,128]{1,0:T(8,128)(2,1)} %param.12, bf16[64,4096]{1,0:T(8,128)(2,1)S(1)} %gather_fusion.2, pred[64]{0:T(512)(128)(4,1)S(1)} %get-tuple-element.18), kind=kOutput, calls=%fused_computation.15 | convolution fusion | flops 67371008 | bytes 1605696 | tf_op jit(solution)/shard_map/dot_general | solution.py:123
  149.3 8.8 %psum.7 = bf16[64,128]{1,0:T(8,128)(2,1)} all-reduce(f32[64,128]{1,0:T(8,128)S(1)} %fusion.3), channel_id=1, replica_groups=mesh['ay'=4,'az'=16,'dp'=4,'tensor'=2] {'tensor'}, use_global_device_ids=true, to_apply=%region_8.10 | all-reduce | flops 8192 | bytes 49152 | tf_op jit(solution)/shard_map/psum | solution.py:124
  (45 shorter events, 1.7 us)
Async XLA Ops:
  0.0 1.3 copy-start
  0.0 2.3 %copy-start.2 = (bf16[64,128]{1,0:T(8,128)(2,1)S(1)}, bf16[64,128]{1,0:T(8,128)(2,1)}, u32[]{:S(2)}) copy-start(bf16[64,128]{1,0:T(8,128)(2,1)} %param.9) | copy-start | bytes 49156
  23.6 15.5 %copy-start.1 = (s32[1,64]{1,0:T(1,128)S(1)}, s32[1,64]{1,0:T(1,128)}, u32[]{:S(2)}) copy-start(s32[1,64]{1,0:T(1,128)} %param.14) | copy-start | bytes 772
  23.6 16.8 %copy-start.3 = (s32[1,64,1]{1,2,0:T(1,128)S(1)}, s32[1,64,1]{1,2,0:T(1,128)}, u32[]{:S(2)}) copy-start(s32[1,64,1]{1,2,0:T(1,128)} %param.15) | copy-start | bytes 772
  24.5 34.2 %all-to-all-start.1 = ((f32[16,40,128]{2,1,0:T(8,128)}), f32[16,40,128]{2,1,0:T(8,128)S(1)}, u32[]{:S(2)}, u32[]{:S(2)}) async-start(f32[16,40,128]{2,1,0:T(8,128)} %bitcast.33), calls=%async_computation.1 | async-start | bytes 655360 | tf_op jit(solution)/shard_map/all_to_all | solution.py:58
  59.9 19.0 %all-to-all-start.2 = ((bf16[16,40,128]{2,1,0:T(8,128)(2,1)}), bf16[16,40,128]{2,1,0:T(8,128)(2,1)S(1)}, u32[]{:S(2)}, u32[]{:S(2)}) async-start(bf16[16,40,128]{2,1,0:T(8,128)(2,1)} %tile.11), calls=%async_computation.2 | async-start | bytes 327680 | tf_op jit(solution)/shard_map/all_to_all | solution.py:33
  79.7 11.1 %all-to-all-start.3 = ((bf16[4,16,40,128]{3,2,1,0:T(8,128)(2,1)}), bf16[4,16,40,128]{3,2,1,0:T(8,128)(2,1)S(1)}, u32[]{:S(2)}, u32[]{:S(2)}) async-start(bf16[4,16,40,128]{3,2,1,0:T(8,128)(2,1)} %tile.12), calls=%async_computation.3 | async-start | bytes 1310720 | tf_op jit(solution)/shard_map/all_to_all | solution.py:34
  122.4 21.1 %all-to-all-start.5 = ((bf16[4,16,16,768]{3,2,1,0:T(8,128)(2,1)}), bf16[4,16,16,768]{3,2,1,0:T(8,128)(2,1)}, u32[]{:S(2)}, u32[]{:S(2)}) async-start(bf16[4,16,16,768]{3,2,1,0:T(8,128)(2,1)} %tile.14), calls=%async_computation.5 | async-start | bytes 3145728 | tf_op jit(solution)/shard_map/all_to_all | solution.py:34

commit v3 on v2

--- a/solution.py
+++ b/solution.py
@@ -116,12 +116,12 @@
         * keyval_mine[:, 1].astype(jnp.float32)[:, :, None, :]
     )
     out_slots = mixed.reshape(CAP, heads_loc * HD).astype(jnp.bfloat16)
-    lanes = out_slots.size // 16
-    gathered = gather_rows(out_slots.reshape(16, lanes), n_y, n_z)
-    gathered = gathered.reshape(-1, heads_loc * HD)
-    heads_out = jnp.take(gathered, owners * CAP + slot_rank, axis=0)
+    slot_rows = heads_loc * HD // 256
+    gathered = gather_rows(out_slots.reshape(CAP * slot_rows, 256), n_y, n_z)
+    gathered = gathered.reshape(-1, slot_rows, 256)
+    heads_out = jnp.take(gathered, owners * CAP + slot_rank, axis=0).reshape(rows_group, -1)
     out_part = jnp.dot(heads_out, w_output, preferred_element_type=jnp.float32)
-    out_total = lax.psum(out_part, "tensor")
+    out_total = out_part + lax.ppermute(out_part, "tensor", [(0, 1), (1, 0)])
     return out_total.astype(jnp.bfloat16)
 
 

time: 159 us -> 154 us (0.969)
  blocking collectives: 57.5 us -> 48.7 us
  starting transfers between devices: 29.3 us -> 35.4 us
  local copies, waits for them, and re-layouts: 13.4 us -> 9.98 us
    psum x1 -> x0, blocking collectives: 8.78 us -> none  [local(): out_total = lax.psum(out_part, 'tensor')]
    ppermute x0 -> x1, starting transfers between devices: none -> 6.86 us  [local(): out_total = out_part + lax.ppermute(out_part, 'tensor', [(0, 1), (1, 0)])]
    another operation x1 -> x0, local copies, waits for them, and re-layouts: 3.26 us -> none  [local(): gathered = gathered.reshape(-1, heads_loc * HD)]
    unnamed x14 -> x15, local copies, waits for them, and re-layouts: 3.8 us -> 3.98 us
  transfers between devices with their start and end apart: 4 -> 5, of which waited for: 4 -> 5; matrix products, arithmetic and copies ran while one was open for 3% -> 3% of each run, Pallas kernels for 0% -> 0%
where the time goes in v3:
time: 154 us; the launch traced here: 153 us
  waiting for transfers between devices  52 us (34%)
  blocking collectives  48.7 us (32%)
  starting transfers between devices  35.4 us (23%)
  local copies, waits for them, and re-layouts  9.98 us (6%)
  matrix products  3.61 us (2%)
  other arithmetic  3.42 us (2%)
    all_to_all x1, blocking collectives, gather_rows(): lax.all_to_all(jnp.tile(rows[None], (n_z, 1, 1)), 'az', 0, 0, tiled=True)  27.7 us
    all_to_all x2, waiting for transfers between devices, gather_rows(): lax.all_to_all(jnp.tile(stage[None], (n_y, 1, 1, 1)), 'ay', 0, 0, tiled=T...  21.9 us
    all_to_all x1, blocking collectives, local(): lax.all_to_all(both.reshape(n_y, per_y, cols), 'ay', 0, 0, tiled=True)  21 us
    all_to_all x1, waiting for transfers between devices, local(): lax.all_to_all(part.reshape(n_z, cols // HD, HD), 'az', 0, 0, tiled=True)  17.9 us
    all_to_all x1, starting transfers between devices, local(): lax.all_to_all(part.reshape(n_z, cols // HD, HD), 'az', 0, 0, tiled=True)  14.7 us
    all_to_all x1, waiting for transfers between devices, gather_rows(): lax.all_to_all(jnp.tile(rows[None], (n_z, 1, 1)), 'az', 0, 0, tiled=True)  11.3 us
    all_to_all x2, starting transfers between devices, gather_rows(): lax.all_to_all(jnp.tile(stage[None], (n_y, 1, 1, 1)), 'ay', 0, 0, tiled=T...  7.04 us
    all_to_all x1, starting transfers between devices, gather_rows(): lax.all_to_all(jnp.tile(rows[None], (n_z, 1, 1)), 'az', 0, 0, tiled=True)  6.86 us
  transfers between devices with their start and end apart: 5, of which 5 were waited for; matrix products, arithmetic and copies ran while one was open for 3% of the time, Pallas kernels for 0%

profile of v3, /device:TPU:35, one launch (start us, length us, event | category | flops | bytes accessed | tf_op | source)
XLA Modules:
  0.0 153.4 jit_solution(16901286444905052357)
XLA Ops:
  0.0 1.1 copy.24
  1.1 0.2 copy-done
  1.3 1.0 fusion.31
  2.6 21.0 %all_to_all.30 = f32[4,16,5120]{2,1,0:T(8,128)S(1)} all-to-all(f32[4,16,5120]{2,1,0:T(8,128)S(1)} %bitcast.109), channel_id=1, replica_groups=mesh['ay'=4,'az'=16,'dp'=4,'tensor'=2] {'ay'}, dimensions={0} | all-to-all | bytes 2621440 | tf_op jit(solution)/shard_map/all_to_all | solution.py:57
  23.7 0.8 copy.25
  24.5 14.7 %all-to-all-start.1 = ((f32[16,40,128]{2,1,0:T(8,128)}), f32[16,40,128]{2,1,0:T(8,128)S(1)}, u32[]{:S(2)}, u32[]{:S(2)}) async-start(f32[16,40,128]{2,1,0:T(8,128)} %bitcast.34), calls=%async_computation.1 | async-start | bytes 655360 | tf_op jit(solution)/shard_map/all_to_all | solution.py:58
  39.2 0.6 fusion.30
  39.7 0.7 fusion.26
  40.8 17.9 %all-to-all-done.1 = f32[16,40,128]{2,1,0:T(8,128)S(1)} async-done(((f32[16,40,128]{2,1,0:T(8,128)}), f32[16,40,128]{2,1,0:T(8,128)S(1)}, u32[]{:S(2)}, u32[]{:S(2)}) %all-to-all-start.1) | async-done | bytes 327712 | tf_op jit(solution)/shard_map/all_to_all | solution.py:58
  59.2 0.7 tile.11
  59.9 6.9 %all-to-all-start.2 = ((bf16[16,40,128]{2,1,0:T(8,128)(2,1)}), bf16[16,40,128]{2,1,0:T(8,128)(2,1)S(1)}, u32[]{:S(2)}, u32[]{:S(2)}) async-start(bf16[16,40,128]{2,1,0:T(8,128)(2,1)} %tile.11), calls=%async_computation.2 | async-start | bytes 327680 | tf_op jit(solution)/shard_map/all_to_all | solution.py:33
  66.7 0.6 gather_fusion.3
  67.5 11.3 %all-to-all-done.2 = bf16[16,40,128]{2,1,0:T(8,128)(2,1)S(1)} async-done(((bf16[16,40,128]{2,1,0:T(8,128)(2,1)}), bf16[16,40,128]{2,1,0:T(8,128)(2,1)S(1)}, u32[]{:S(2)}, u32[]{:S(2)}) %all-to-all-start.2) | async-done | bytes 163872 | tf_op jit(solution)/shard_map/all_to_all | solution.py:33
  78.8 0.9 tile.12
  79.7 3.5 %all-to-all-start.3 = ((bf16[4,16,40,128]{3,2,1,0:T(8,128)(2,1)}), bf16[4,16,40,128]{3,2,1,0:T(8,128)(2,1)S(1)}, u32[]{:S(2)}, u32[]{:S(2)}) async-start(bf16[4,16,40,128]{3,2,1,0:T(8,128)(2,1)} %tile.12), calls=%async_computation.3 | async-start | bytes 1310720 | tf_op jit(solution)/shard_map/all_to_all | solution.py:34
  83.2 0.6 gather_fusion.4
  83.9 1.6 %copy.57 = bf16[1,768,2,4,128]{4,1,3,2,0:T(8,128)(2,1)S(1)} copy(bf16[1,768,2,4,128]{4,3,2,1,0:T(4,128)(2,1)} %param.13) | data formatting | bytes 3145728 | tf_op args[4]
  85.6 5.2 %all-to-all-done.3 = bf16[4,16,40,128]{3,2,1,0:T(8,128)(2,1)S(1)} async-done(((bf16[4,16,40,128]{3,2,1,0:T(8,128)(2,1)}), bf16[4,16,40,128]{3,2,1,0:T(8,128)(2,1)S(1)}, u32[]{:S(2)}, u32[]{:S(2)}) %all-to-all-start.3) | async-done | bytes 655392 | tf_op jit(solution)/shard_map/all_to_all | solution.py:34
  91.0 0.6 gather_fusion
  91.6 0.6 gather_fusion.1
  92.4 0.4 select_reduce_fusion
  92.8 0.2 fusion.7
  93.1 0.3 fusion.2
  93.4 27.7 %all_to_all.31 = bf16[16,48,256]{2,1,0:T(8,128)(2,1)S(1)} all-to-all(bf16[16,48,256]{2,1,0:T(8,128)(2,1)S(1)} %tile.13), channel_id=1, replica_groups=mesh['ay'=4,'az'=16,'dp'=4,'tensor'=2] {'az'}, dimensions={0} | all-to-all | bytes 786432 | tf_op jit(solution)/shard_map/all_to_all | solution.py:33
  121.1 1.3 tile.14
  122.4 3.6 %all-to-all-start.5 = ((bf16[4,16,48,256]{3,2,1,0:T(8,128)(2,1)}), bf16[4,16,48,256]{3,2,1,0:T(8,128)(2,1)S(1)}, u32[]{:S(2)}, u32[]{:S(2)}) async-start(bf16[4,16,48,256]{3,2,1,0:T(8,128)(2,1)} %tile.14), calls=%async_computation.5 | async-start | bytes 3145728 | tf_op jit(solution)/shard_map/all_to_all | solution.py:34
  126.0 16.7 %all-to-all-done.5 = bf16[4,16,48,256]{3,2,1,0:T(8,128)(2,1)S(1)} async-done(((bf16[4,16,48,256]{3,2,1,0:T(8,128)(2,1)}), bf16[4,16,48,256]{3,2,1,0:T(8,128)(2,1)S(1)}, u32[]{:S(2)}, u32[]{:S(2)}) %all-to-all-start.5) | async-done | bytes 1572896 | tf_op jit(solution)/shard_map/all_to_all | solution.py:34
  142.6 0.6 gather_fusion.2
  143.4 1.6 %fusion.3 = f32[64,128]{1,0:T(8,128)S(1)} fusion(bf16[4096,128]{1,0:T(8,128)(2,1)} %param.12, bf16[64,4096]{1,0:T(8,128)(2,1)S(1)} %bitcast.119, pred[64]{0:T(512)(128)(4,1)S(1)} %get-tuple-element.18), kind=kOutput, calls=%fused_computation.15 | convolution fusion | flops 67371008 | bytes 1605696 | tf_op jit(solution)/shard_map/dot_general | solution.py:123
  145.0 6.9 %collective-permute-start = (f32[64,128]{1,0:T(8,128)S(1)}, f32[64,128]{1,0:T(8,128)S(1)}, u32[]{:S(2)}, u32[]{:S(2)}) collective-permute-start(f32[64,128]{1,0:T(8,128)S(1)} %fusion.3), channel_id=1, source_target_pairs={{0,1},{1,0},{2,3},{3,2},{4,5},{5,4},{6,7},{7,6},{8,9},{9,8},{10,11... | collective-permute-start | bytes 98312 | tf_op jit(solution)/shard_map/ppermute | solution.py:124
  151.9 0.8 collective-permute-done
  152.8 0.6 add_convert_fusion
  (47 shorter events, 2.0 us)
Async XLA Ops:
  0.0 1.3 copy-start
  0.0 2.3 %copy-start.2 = (bf16[64,128]{1,0:T(8,128)(2,1)S(1)}, bf16[64,128]{1,0:T(8,128)(2,1)}, u32[]{:S(2)}) copy-start(bf16[64,128]{1,0:T(8,128)(2,1)} %param.9) | copy-start | bytes 49156
  23.6 15.5 %copy-start.1 = (s32[1,64]{1,0:T(1,128)S(1)}, s32[1,64]{1,0:T(1,128)}, u32[]{:S(2)}) copy-start(s32[1,64]{1,0:T(1,128)} %param.14) | copy-start | bytes 772
  23.6 16.8 %copy-start.3 = (s32[1,64,1]{1,2,0:T(1,128)S(1)}, s32[1,64,1]{1,2,0:T(1,128)}, u32[]{:S(2)}) copy-start(s32[1,64,1]{1,2,0:T(1,128)} %param.15) | copy-start | bytes 772
  24.5 34.2 %all-to-all-start.1 = ((f32[16,40,128]{2,1,0:T(8,128)}), f32[16,40,128]{2,1,0:T(8,128)S(1)}, u32[]{:S(2)}, u32[]{:S(2)}) async-start(f32[16,40,128]{2,1,0:T(8,128)} %bitcast.34), calls=%async_computation.1 | async-start | bytes 655360 | tf_op jit(solution)/shard_map/all_to_all | solution.py:58
  59.9 19.0 %all-to-all-start.2 = ((bf16[16,40,128]{2,1,0:T(8,128)(2,1)}), bf16[16,40,128]{2,1,0:T(8,128)(2,1)S(1)}, u32[]{:S(2)}, u32[]{:S(2)}) async-start(bf16[16,40,128]{2,1,0:T(8,128)(2,1)} %tile.11), calls=%async_computation.2 | async-start | bytes 327680 | tf_op jit(solution)/shard_map/all_to_all | solution.py:33
  79.7 11.1 %all-to-all-start.3 = ((bf16[4,16,40,128]{3,2,1,0:T(8,128)(2,1)}), bf16[4,16,40,128]{3,2,1,0:T(8,128)(2,1)S(1)}, u32[]{:S(2)}, u32[]{:S(2)}) async-start(bf16[4,16,40,128]{3,2,1,0:T(8,128)(2,1)} %tile.12), calls=%async_computation.3 | async-start | bytes 1310720 | tf_op jit(solution)/shard_map/all_to_all | solution.py:34
  122.4 20.2 %all-to-all-start.5 = ((bf16[4,16,48,256]{3,2,1,0:T(8,128)(2,1)}), bf16[4,16,48,256]{3,2,1,0:T(8,128)(2,1)S(1)}, u32[]{:S(2)}, u32[]{:S(2)}) async-start(bf16[4,16,48,256]{3,2,1,0:T(8,128)(2,1)} %tile.14), calls=%async_computation.5 | async-start | bytes 3145728 | tf_op jit(solution)/shard_map/all_to_all | solution.py:34
  145.0 7.7 %collective-permute-start = (f32[64,128]{1,0:T(8,128)S(1)}, f32[64,128]{1,0:T(8,128)S(1)}, u32[]{:S(2)}, u32[]{:S(2)}) collective-permute-start(f32[64,128]{1,0:T(8,128)S(1)} %fusion.3), channel_id=1, source_target_pairs={{0,1},{1,0},{2,3},{3,2},{4,5},{5,4},{6,7},{7,6},{8,9},{9,8},{10,11... | collective-permute-start | bytes 98312 | tf_op jit(solution)/shard_map/ppermute | solution.py:124

commit v4 on v3

--- a/solution.py
+++ b/solution.py
@@ -68,9 +68,10 @@
     row_bf = jnp.concatenate(
         [q_rot.reshape(1, q_cols), k_rot.reshape(1, kv_cols), v_new.reshape(1, kv_cols)], axis=1
     )
-    all_rows = gather_rows(row_bf.reshape(cols // HD, HD), n_y, n_z).reshape(-1, cols)
-    query_rows = all_rows[:, :q_cols]
-    keyval_rows = all_rows[:, q_cols:]
+    tiles = cols // HD
+    rows_z = lax.all_to_all(
+        jnp.tile(row_bf.reshape(1, tiles, HD), (n_z, 1, 1)), "az", 0, 0, tiled=True
+    ).reshape(n_z, cols)
     req_order = jnp.arange(rows_group, dtype=jnp.int32)
     same_owner = owners[:, None] == owners[None, :]
     earlier = req_order[None, :] < req_order[:, None]
@@ -84,8 +85,16 @@
     present = jnp.any(slot_hit, axis=1)
     my_start = jnp.take(starts, chosen)
     my_len = jnp.where(present, jnp.take(req_lens, chosen), 0)
-    query_mine = jnp.take(query_rows, chosen, axis=0)
-    keyval_mine = jnp.take(keyval_rows, chosen, axis=0).reshape(CAP, 2, kv_loc, HD)
+    dest_owner = jnp.arange(n_y, dtype=jnp.int32) * n_z + lax.axis_index("az")
+    dest_hit = (owners[None, None, :] == dest_owner[:, None, None]) & (
+        slot_rank[None, None, :] == jnp.arange(CAP, dtype=jnp.int32)[None, :, None]
+    )
+    dest_req = jnp.sum(jnp.where(dest_hit, req_order[None, None, :], 0), axis=2)
+    send = jnp.take(rows_z, dest_req % n_z, axis=0).reshape(n_y, CAP * tiles, HD)
+    recv = lax.all_to_all(send, "ay", 0, 0, tiled=True).reshape(n_y, CAP, cols)
+    mine_rows = recv[chosen // n_z, jnp.arange(CAP)]
+    query_mine = mine_rows[:, :q_cols]
+    keyval_mine = mine_rows[:, q_cols:].reshape(CAP, 2, kv_loc, HD)
     cache_local = kv_cache[0]
     grouped = query_mine.reshape(CAP, kv_loc, group_size, HD)
     scores = (

time: 154 us -> 151 us (0.981)
  the two profiles are of different devices: /device:TPU:35 before, /device:TPU:39 now
where the time goes in v4:
time: 151 us
  waiting for transfers between devices  65.5 us (43%)
  starting transfers between devices  39.6 us (26%)
  blocking collectives  26.3 us (17%)
  local copies, waits for them, and re-layouts  9.93 us (7%)
  other arithmetic  5.37 us (4%)
  matrix products  3.58 us (2%)
    all_to_all x1, blocking collectives, gather_rows(): lax.all_to_all(jnp.tile(rows[None], (n_z, 1, 1)), 'az', 0, 0, tiled=True)  26.3 us
    all_to_all x1, waiting for transfers between devices, local(): lax.all_to_all(part.reshape(n_z, cols // HD, HD), 'az', 0, 0, tiled=True)  18.4 us
    all_to_all x1, waiting for transfers between devices, gather_rows(): lax.all_to_all(jnp.tile(stage[None], (n_y, 1, 1, 1)), 'ay', 0, 0, tiled=T...  16.7 us
    all_to_all x1, waiting for transfers between devices, local(): lax.all_to_all(both.reshape(n_y, per_y, cols), 'ay', 0, 0, tiled=True)  16.1 us
    all_to_all x1, starting transfers between devices, local(): lax.all_to_all(part.reshape(n_z, cols // HD, HD), 'az', 0, 0, tiled=True)  14.7 us
    all_to_all x1, waiting for transfers between devices, local(): lax.all_to_all(jnp.tile(row_bf.reshape(1, tiles, HD), (n_z, 1, 1)), 'az',...  10.3 us
    ppermute x1, starting transfers between devices, local(): out_total = out_part + lax.ppermute(out_part, 'tensor', [(0, 1), (1, 0)])  6.87 us
    all_to_all x1, starting transfers between devices, local(): lax.all_to_all(jnp.tile(row_bf.reshape(1, tiles, HD), (n_z, 1, 1)), 'az',...  6.86 us
  transfers between devices with their start and end apart: 6, of which 6 were waited for; matrix products, arithmetic and copies ran while one was open for 4% of the time, Pallas kernels for 0%

profile of v4, /device:TPU:39, one launch (start us, length us, event | category | flops | bytes accessed | tf_op | source)
XLA Modules:
  0.0 150.5 jit_solution(759788263155746986)
XLA Ops:
  0.0 1.1 copy.26
  1.3 1.0 fusion.34
  2.5 1.2 pad_maximum_fusion
  3.7 4.3 %all-to-all-start = ((f32[4,16,5120]{2,1,0:T(8,128)}), f32[4,16,5120]{2,1,0:T(8,128)S(1)}, u32[]{:S(2)}, u32[]{:S(2)}) async-start(f32[4,16,5120]{2,1,0:T(8,128)} %bitcast.128), calls=%async_computation | async-start | bytes 2621440 | tf_op jit(solution)/shard_map/all_to_all | solution.py:57
  8.0 0.6 fusion.33
  8.9 16.1 %all-to-all-done = f32[4,16,5120]{2,1,0:T(8,128)S(1)} async-done(((f32[4,16,5120]{2,1,0:T(8,128)}), f32[4,16,5120]{2,1,0:T(8,128)S(1)}, u32[]{:S(2)}, u32[]{:S(2)}) %all-to-all-start) | async-done | bytes 1310752 | tf_op jit(solution)/shard_map/all_to_all | solution.py:57
  25.1 0.8 copy.27
  25.9 14.7 %all-to-all-start.1 = ((f32[16,40,128]{2,1,0:T(8,128)}), f32[16,40,128]{2,1,0:T(8,128)S(1)}, u32[]{:S(2)}, u32[]{:S(2)}) async-start(f32[16,40,128]{2,1,0:T(8,128)} %bitcast.35), calls=%async_computation.1 | async-start | bytes 655360 | tf_op jit(solution)/shard_map/all_to_all | solution.py:58
  40.9 0.7 fusion.29
  41.7 18.4 %all-to-all-done.1 = f32[16,40,128]{2,1,0:T(8,128)S(1)} async-done(((f32[16,40,128]{2,1,0:T(8,128)}), f32[16,40,128]{2,1,0:T(8,128)S(1)}, u32[]{:S(2)}, u32[]{:S(2)}) %all-to-all-start.1) | async-done | bytes 327712 | tf_op jit(solution)/shard_map/all_to_all | solution.py:58
  60.6 0.7 tile.9
  61.3 6.9 %all-to-all-start.2 = ((bf16[16,40,128]{2,1,0:T(8,128)(2,1)}), bf16[16,40,128]{2,1,0:T(8,128)(2,1)S(1)}, u32[]{:S(2)}, u32[]{:S(2)}) async-start(bf16[16,40,128]{2,1,0:T(8,128)(2,1)} %tile.9), calls=%async_computation.2 | async-start | bytes 327680 | tf_op jit(solution)/shard_map/all_to_all | solution.py:72
  68.5 0.6 gather_fusion.4
  69.1 0.6 gather_fusion.3
  69.9 10.3 %all-to-all-done.2 = bf16[16,40,128]{2,1,0:T(8,128)(2,1)S(1)} async-done(((bf16[16,40,128]{2,1,0:T(8,128)(2,1)}), bf16[16,40,128]{2,1,0:T(8,128)(2,1)S(1)}, u32[]{:S(2)}, u32[]{:S(2)}) %all-to-all-start.2) | async-done | bytes 163872 | tf_op jit(solution)/shard_map/all_to_all | solution.py:72
  80.3 0.6 gather_fusion
  81.0 0.8 broadcast_select_fusion
  81.8 3.3 %all-to-all-start.3 = ((bf16[4,120,128]{2,1,0:T(8,128)(2,1)}), bf16[4,120,128]{2,1,0:T(8,128)(2,1)S(1)}, u32[]{:S(2)}, u32[]{:S(2)}) async-start(bf16[4,120,128]{2,1,0:T(8,128)(2,1)} %broadcast_select_fusion), calls=%async_computation.3 | async-start | bytes 245760 | tf_op jit(solution)/shard_map/all_to_all | solution.py:94
  85.1 1.6 %copy.64 = bf16[1,768,2,4,128]{4,1,3,2,0:T(8,128)(2,1)S(1)} copy(bf16[1,768,2,4,128]{4,3,2,1,0:T(4,128)(2,1)} %param.13) | data formatting | bytes 3145728 | tf_op args[4]
  86.7 3.1 %all-to-all-done.3 = bf16[4,120,128]{2,1,0:T(8,128)(2,1)S(1)} async-done(((bf16[4,120,128]{2,1,0:T(8,128)(2,1)}), bf16[4,120,128]{2,1,0:T(8,128)(2,1)S(1)}, u32[]{:S(2)}, u32[]{:S(2)}) %all-to-all-start.3) | async-done | bytes 122912 | tf_op jit(solution)/shard_map/all_to_all | solution.py:94
  90.0 0.8 gather_fusion.1
  90.9 0.4 select_reduce_fusion
  91.6 0.3 fusion.2
  92.0 26.3 %all_to_all.30 = bf16[16,48,256]{2,1,0:T(8,128)(2,1)S(1)} all-to-all(bf16[16,48,256]{2,1,0:T(8,128)(2,1)S(1)} %tile.10), channel_id=1, replica_groups=mesh['ay'=4,'az'=16,'dp'=4,'tensor'=2] {'az'}, dimensions={0} | all-to-all | bytes 786432 | tf_op jit(solution)/shard_map/all_to_all | solution.py:33
  118.3 1.3 tile.11
  119.6 3.6 %all-to-all-start.5 = ((bf16[4,16,48,256]{3,2,1,0:T(8,128)(2,1)}), bf16[4,16,48,256]{3,2,1,0:T(8,128)(2,1)S(1)}, u32[]{:S(2)}, u32[]{:S(2)}) async-start(bf16[4,16,48,256]{3,2,1,0:T(8,128)(2,1)} %tile.11), calls=%async_computation.5 | async-start | bytes 3145728 | tf_op jit(solution)/shard_map/all_to_all | solution.py:34
  123.1 16.7 %all-to-all-done.5 = bf16[4,16,48,256]{3,2,1,0:T(8,128)(2,1)S(1)} async-done(((bf16[4,16,48,256]{3,2,1,0:T(8,128)(2,1)}), bf16[4,16,48,256]{3,2,1,0:T(8,128)(2,1)S(1)}, u32[]{:S(2)}, u32[]{:S(2)}) %all-to-all-start.5) | async-done | bytes 1572896 | tf_op jit(solution)/shard_map/all_to_all | solution.py:34
  139.8 0.6 gather_fusion.2
  140.6 1.6 %fusion.3 = f32[64,128]{1,0:T(8,128)S(1)} fusion(bf16[4096,128]{1,0:T(8,128)(2,1)} %param.12, bf16[64,4096]{1,0:T(8,128)(2,1)S(1)} %bitcast.136, pred[64]{0:T(512)(128)(4,1)S(1)} %get-tuple-element.16), kind=kOutput, calls=%fused_computation.14 | convolution fusion | flops 67371008 | bytes 1605696 | tf_op jit(solution)/shard_map/dot_general | solution.py:132
  142.2 6.9 %collective-permute-start = (f32[64,128]{1,0:T(8,128)S(1)}, f32[64,128]{1,0:T(8,128)S(1)}, u32[]{:S(2)}, u32[]{:S(2)}) collective-permute-start(f32[64,128]{1,0:T(8,128)S(1)} %fusion.3), channel_id=1, source_target_pairs={{0,1},{1,0},{2,3},{3,2},{4,5},{5,4},{6,7},{7,6},{8,9},{9,8},{10,11... | collective-permute-start | bytes 98312 | tf_op jit(solution)/shard_map/ppermute | solution.py:133
  149.1 0.8 collective-permute-done
  149.9 0.6 add_convert_fusion
  (60 shorter events, 3.1 us)
Async XLA Ops:
  0.0 1.3 copy-start
  0.0 2.3 %copy-start.2 = (bf16[64,128]{1,0:T(8,128)(2,1)S(1)}, bf16[64,128]{1,0:T(8,128)(2,1)}, u32[]{:S(2)}) copy-start(bf16[64,128]{1,0:T(8,128)(2,1)} %param.9) | copy-start | bytes 49156
  3.7 4.3 %copy-start.1 = (s32[1,64]{1,0:T(1,128)S(1)}, s32[1,64]{1,0:T(1,128)}, u32[]{:S(2)}) copy-start(s32[1,64]{1,0:T(1,128)} %param.14) | copy-start | bytes 772
  3.7 4.9 %copy-start.3 = (s32[1,64,1]{1,2,0:T(1,128)S(1)}, s32[1,64,1]{1,2,0:T(1,128)}, u32[]{:S(2)}) copy-start(s32[1,64,1]{1,2,0:T(1,128)} %param.15) | copy-start | bytes 772
  3.7 21.4 %all-to-all-start = ((f32[4,16,5120]{2,1,0:T(8,128)}), f32[4,16,5120]{2,1,0:T(8,128)S(1)}, u32[]{:S(2)}, u32[]{:S(2)}) async-start(f32[4,16,5120]{2,1,0:T(8,128)} %bitcast.128), calls=%async_computation | async-start | bytes 2621440 | tf_op jit(solution)/shard_map/all_to_all | solution.py:57
  25.9 34.2 %all-to-all-start.1 = ((f32[16,40,128]{2,1,0:T(8,128)}), f32[16,40,128]{2,1,0:T(8,128)S(1)}, u32[]{:S(2)}, u32[]{:S(2)}) async-start(f32[16,40,128]{2,1,0:T(8,128)} %bitcast.35), calls=%async_computation.1 | async-start | bytes 655360 | tf_op jit(solution)/shard_map/all_to_all | solution.py:58
  61.3 19.0 %all-to-all-start.2 = ((bf16[16,40,128]{2,1,0:T(8,128)(2,1)}), bf16[16,40,128]{2,1,0:T(8,128)(2,1)S(1)}, u32[]{:S(2)}, u32[]{:S(2)}) async-start(bf16[16,40,128]{2,1,0:T(8,128)(2,1)} %tile.9), calls=%async_computation.2 | async-start | bytes 327680 | tf_op jit(solution)/shard_map/all_to_all | solution.py:72
  81.8 8.1 %all-to-all-start.3 = ((bf16[4,120,128]{2,1,0:T(8,128)(2,1)}), bf16[4,120,128]{2,1,0:T(8,128)(2,1)S(1)}, u32[]{:S(2)}, u32[]{:S(2)}) async-start(bf16[4,120,128]{2,1,0:T(8,128)(2,1)} %broadcast_select_fusion), calls=%async_computation.3 | async-start | bytes 245760 | tf_op jit(solution)/shard_map/all_to_all | solution.py:94
  119.6 20.2 %all-to-all-start.5 = ((bf16[4,16,48,256]{3,2,1,0:T(8,128)(2,1)}), bf16[4,16,48,256]{3,2,1,0:T(8,128)(2,1)S(1)}, u32[]{:S(2)}, u32[]{:S(2)}) async-start(bf16[4,16,48,256]{3,2,1,0:T(8,128)(2,1)} %tile.11), calls=%async_computation.5 | async-start | bytes 3145728 | tf_op jit(solution)/shard_map/all_to_all | solution.py:34
  142.2 7.7 %collective-permute-start = (f32[64,128]{1,0:T(8,128)S(1)}, f32[64,128]{1,0:T(8,128)S(1)}, u32[]{:S(2)}, u32[]{:S(2)}) collective-permute-start(f32[64,128]{1,0:T(8,128)S(1)} %fusion.3), channel_id=1, source_target_pairs={{0,1},{1,0},{2,3},{3,2},{4,5},{5,4},{6,7},{7,6},{8,9},{9,8},{10,11... | collective-permute-start | bytes 98312 | tf_op jit(solution)/shard_map/ppermute | solution.py:133
